TPU v7x, 32 devices: a whole 2x2x4 slice. The times are simulated.
32 devices in a mesh: outer: 4 (over z), inner: 2 (over x), tensor: 4 (over y, core).
Axes of the slice: x: 2, y: 2, z: 4, core: 2. Of those that a mesh axis runs over, the one named last changes fastest.
Arguments:
- hidden_in: bfloat16 [16, 577, 1024], P(('outer', 'inner')), may hold values from -6 to 6
- ln1_gain: float32 [1024], replicated, may hold values from 0.5 to 1.5
- ln1_shift: float32 [1024], replicated, may hold values from -1.5 to 1.5
- w_qkv: bfloat16 [1024, 3, 1024], P(None, None, 'tensor'), may hold values from -0.1875 to 0.1875
- qkv_bias: float32 [2, 1024], P(None, 'tensor'), may hold values from -1.5 to 1.5
- w_out: bfloat16 [1024, 1024], P('tensor'), may hold values from -0.75 to 0.75
- out_bias: float32 [1024], replicated, may hold values from -1.5 to 1.5
- ln2_gain: float32 [1024], replicated, may hold values from 0.5 to 1.5
- ln2_shift: float32 [1024], replicated, may hold values from -1.5 to 1.5
- w_fc1: bfloat16 [1024, 4096], P(None, 'tensor'), may hold values from -0.1875 to 0.1875
- fc1_bias: float32 [4096], P('tensor'), may hold values from -1.5 to 1.5
- w_fc2: bfloat16 [4096, 1024], P('tensor'), may hold values from -0.09375 to 0.09375
- fc2_bias: float32 [1024], replicated, may hold values from -1.5 to 1.5
- flags: int32 [16], P(('outer', 'inner')), may hold values 0 or 1
- out_grad: bfloat16 [16, 577, 1024], P(('outer', 'inner')), may hold values from -6 to 6
Outputs:
- block_out: bfloat16 [16, 577, 1024], P(('outer', 'inner'))
- in_grad: bfloat16 [16, 577, 1024], P(('outer', 'inner'))
- g_ln1_gain: float32 [1024], replicated
- g_ln1_shift: float32 [1024], replicated
- g_w_qkv: float32 [1024, 3, 1024], P(None, None, 'tensor')
- g_qkv_bias: float32 [2, 1024], P(None, 'tensor')
- g_w_out: float32 [1024, 1024], P('tensor')
- g_out_bias: float32 [1024], replicated
- g_ln2_gain: float32 [1024], replicated
- g_ln2_shift: float32 [1024], replicated
- g_w_fc1: float32 [1024, 4096], P(None, 'tensor')
- g_fc1_bias: float32 [4096], P('tensor')
- g_w_fc2: float32 [4096, 1024], P('tensor')
- g_fc2_bias: float32 [1024], replicated
Inputs may be any that keep to these rules, and one draw needn't show every extreme that they name: `flags`: 1 marks an image, 0 a padded slot.
All inputs are finite; a program needn't handle non-finite values. No bound on the sum of `flags` on one device may be relied on, other than what follows from the above.
Results may differ from a plain program's by a relative error of at most 0.012.
Values sent between devices are 32-bit elements; how exact they have to be, the bound alone decides.
No kernel may reach another device: no remote copies, remote signals or barrier semaphores. Data moves between devices by JAX's collectives and lax.ppermute only.
A program may use at most 192 MiB of HBM per device.

v0:
```python
import jax
import jax.numpy as jnp
from jax import lax
from jax.sharding import PartitionSpec as P

HD = 64
norm_eps = 1e-05


def layer_norm(values_in, gain_vec, shift_vec):
    row_mean = jnp.mean(values_in, axis=-1, keepdims=True)
    centered = values_in - row_mean
    row_var = jnp.mean(centered * centered, axis=-1, keepdims=True)
    return centered * lax.rsqrt(row_var + norm_eps) * gain_vec + shift_vec


def quick_gelu(values_in):
    return values_in * jax.nn.sigmoid(1.702 * values_in)


def gelu_slope(values_in):
    sig_val = jax.nn.sigmoid(1.702 * values_in)
    return sig_val + 1.702 * values_in * sig_val * (1.0 - sig_val)


def mat_prod(left, right):
    return jnp.dot(left, right, preferred_element_type=jnp.float32)


def left_contract(left, right):
    return lax.dot_general(
        left, right, (((0,), (0,)), ((), ())), preferred_element_type=jnp.float32
    )


def right_contract(left, right):
    return lax.dot_general(
        left, right, (((1,), (1,)), ((), ())), preferred_element_type=jnp.float32
    )


def col_sum(values_in):
    return jnp.sum(values_in.astype(jnp.float32), axis=0)


def attn_scores(q_heads, k_heads, score_scale):
    return (
        jnp.einsum("bqhd,bkhd->bhqk", q_heads, k_heads, preferred_element_type=jnp.float32)
        * score_scale
    )


def per_device(
    hidden_in,
    ln1_gain,
    ln1_shift,
    w_qkv,
    qkv_bias,
    w_out,
    out_bias,
    ln2_gain,
    ln2_shift,
    w_fc1,
    fc1_bias,
    w_fc2,
    fc2_bias,
    flags,
    out_grad,
):
    img_count, seq_len, model_width = hidden_in.shape
    row_count = img_count * seq_len
    head_cols = w_qkv.shape[2]
    head_count = head_cols // HD
    score_scale = HD ** (-0.5)
    head_shape = (img_count, seq_len, head_count, HD)
    qkv_flat = w_qkv.reshape(model_width, 3 * head_cols)
    x_rows = hidden_in.reshape(row_count, model_width).astype(jnp.float32)
    normed1 = layer_norm(x_rows, ln1_gain, ln1_shift).astype(jnp.bfloat16)
    projected = mat_prod(normed1, qkv_flat).reshape(row_count, 3, head_cols)
    q_heads = (projected[:, 0] + qkv_bias[0]).astype(jnp.bfloat16).reshape(head_shape)
    k_heads = projected[:, 1].astype(jnp.bfloat16).reshape(head_shape)
    v_heads = (projected[:, 2] + qkv_bias[1]).astype(jnp.bfloat16).reshape(head_shape)
    scores = attn_scores(q_heads, k_heads, score_scale)
    log_total = jax.nn.logsumexp(scores, axis=-1, keepdims=True)
    attn_probs = jnp.exp(scores - log_total).astype(jnp.bfloat16)
    attended = jnp.einsum(
        "bhqk,bkhd->bqhd", attn_probs, v_heads, preferred_element_type=jnp.float32
    )
    attended = attended.astype(jnp.bfloat16).reshape(row_count, head_cols)
    attn_total = lax.psum(mat_prod(attended, w_out), "tensor")
    resid_mid = x_rows + attn_total + out_bias
    normed2 = layer_norm(resid_mid, ln2_gain, ln2_shift).astype(jnp.bfloat16)
    pre_act = mat_prod(normed2, w_fc1) + fc1_bias
    gelu_out = quick_gelu(pre_act).astype(jnp.bfloat16)
    mlp_total = lax.psum(mat_prod(gelu_out, w_fc2), "tensor")
    block_out = (resid_mid + mlp_total + fc2_bias).astype(jnp.bfloat16).reshape(hidden_in.shape)
    out_cot = (out_grad.astype(jnp.float32) * flags.astype(jnp.float32)[:, None, None]).reshape(
        row_count, model_width
    )
    g_fc2_bias = jnp.sum(out_cot, axis=0)
    mlp_cot = out_cot.astype(jnp.bfloat16)
    g_w_fc2 = left_contract(gelu_out, mlp_cot)
    pre_grad = (right_contract(mlp_cot, w_fc2) * gelu_slope(pre_act)).astype(jnp.bfloat16)
    g_w_fc1 = left_contract(normed2, pre_grad)
    g_fc1_bias = col_sum(pre_grad)
    norm2_grad = lax.psum(right_contract(pre_grad, w_fc1), "tensor")
    unused_two, norm2_pull = jax.vjp(layer_norm, resid_mid, ln2_gain, ln2_shift)
    mid_from_norm, g_ln2_gain, g_ln2_shift = norm2_pull(norm2_grad)
    resid_grad = out_cot + mid_from_norm
    g_out_bias = jnp.sum(resid_grad, axis=0)
    attn_cot = resid_grad.astype(jnp.bfloat16)
    g_w_out = left_contract(attended, attn_cot)
    attended_grad = right_contract(attn_cot, w_out).astype(jnp.bfloat16).reshape(head_shape)
    again = attn_scores(q_heads, k_heads, score_scale)
    probs_again = jnp.exp(again - log_total)
    probs_low = probs_again.astype(jnp.bfloat16)
    probs_grad = jnp.einsum(
        "bqhd,bkhd->bhqk", attended_grad, v_heads, preferred_element_type=jnp.float32
    )
    row_dot = jnp.sum(probs_again * probs_grad, axis=-1, keepdims=True)
    score_grad = (probs_again * (probs_grad - row_dot)).astype(jnp.bfloat16)
    q_grad = (
        jnp.einsum("bhqk,bkhd->bqhd", score_grad, k_heads, preferred_element_type=jnp.float32)
        * score_scale
    ).astype(jnp.bfloat16)
    k_grad = (
        jnp.einsum("bhqk,bqhd->bkhd", score_grad, q_heads, preferred_element_type=jnp.float32)
        * score_scale
    ).astype(jnp.bfloat16)
    v_grad = jnp.einsum(
        "bhqk,bqhd->bkhd", probs_low, attended_grad, preferred_element_type=jnp.float32
    ).astype(jnp.bfloat16)
    q_rows = q_grad.reshape(row_count, head_cols)
    v_rows = v_grad.reshape(row_count, head_cols)
    qkv_grad = jnp.stack([q_rows, k_grad.reshape(row_count, head_cols), v_rows], axis=1).reshape(
        row_count, 3 * head_cols
    )
    g_w_qkv = left_contract(normed1, qkv_grad).reshape(model_width, 3, head_cols)
    g_qkv_bias = jnp.stack([col_sum(q_rows), col_sum(v_rows)], axis=0)
    norm1_grad = lax.psum(right_contract(qkv_grad, qkv_flat), "tensor")
    unused_one, norm1_pull = jax.vjp(layer_norm, x_rows, ln1_gain, ln1_shift)
    x_from_norm, g_ln1_gain, g_ln1_shift = norm1_pull(norm1_grad)
    in_grad = (resid_grad + x_from_norm).astype(jnp.bfloat16).reshape(hidden_in.shape)
    shares = (
        lax.psum_scatter(g_ln1_gain, "inner", scatter_dimension=0, tiled=True),
        lax.psum_scatter(g_ln1_shift, "inner", scatter_dimension=0, tiled=True),
        lax.psum_scatter(g_w_qkv, "inner", scatter_dimension=0, tiled=True),
        lax.psum_scatter(g_qkv_bias, "inner", scatter_dimension=1, tiled=True),
        lax.psum_scatter(g_w_out, "inner", scatter_dimension=1, tiled=True),
        lax.psum_scatter(g_out_bias, "inner", scatter_dimension=0, tiled=True),
        lax.psum_scatter(g_ln2_gain, "inner", scatter_dimension=0, tiled=True),
        lax.psum_scatter(g_ln2_shift, "inner", scatter_dimension=0, tiled=True),
        lax.psum_scatter(g_w_fc1, "inner", scatter_dimension=0, tiled=True),
        lax.psum_scatter(g_fc1_bias, "inner", scatter_dimension=0, tiled=True),
        lax.psum_scatter(g_w_fc2, "inner", scatter_dimension=1, tiled=True),
        lax.psum_scatter(g_fc2_bias, "inner", scatter_dimension=0, tiled=True),
    )
    shares = lax.psum(
        (
            shares[0],
            shares[1],
            shares[2],
            shares[3],
            shares[4],
            shares[5],
            shares[6],
            shares[7],
            shares[8],
            shares[9],
            shares[10],
            shares[11],
        ),
        "outer",
    )
    (
        s_ln1_gain,
        s_ln1_shift,
        s_w_qkv,
        s_qkv_bias,
        s_w_out,
        s_out_bias,
        s_ln2_gain,
        s_ln2_shift,
        s_w_fc1,
        s_fc1_bias,
        s_w_fc2,
        s_fc2_bias,
    ) = shares
    summed = (
        lax.all_gather(s_ln1_gain, "inner", axis=0, tiled=True),
        lax.all_gather(s_ln1_shift, "inner", axis=0, tiled=True),
        lax.all_gather(s_w_qkv, "inner", axis=0, tiled=True),
        lax.all_gather(s_qkv_bias, "inner", axis=1, tiled=True),
        lax.all_gather(s_w_out, "inner", axis=1, tiled=True),
        lax.all_gather(s_out_bias, "inner", axis=0, tiled=True),
        lax.all_gather(s_ln2_gain, "inner", axis=0, tiled=True),
        lax.all_gather(s_ln2_shift, "inner", axis=0, tiled=True),
        lax.all_gather(s_w_fc1, "inner", axis=0, tiled=True),
        lax.all_gather(s_fc1_bias, "inner", axis=0, tiled=True),
        lax.all_gather(s_w_fc2, "inner", axis=1, tiled=True),
        lax.all_gather(s_fc2_bias, "inner", axis=0, tiled=True),
    )
    return (
        block_out,
        in_grad,
        summed[0],
        summed[1],
        summed[2],
        summed[3],
        summed[4],
        summed[5],
        summed[6],
        summed[7],
        summed[8],
        summed[9],
        summed[10],
        summed[11],
    )


def solution(mesh):
    placed = (
        P(("outer", "inner"), None, None),
        P(),
        P(),
        P(None, None, "tensor"),
        P(None, "tensor"),
        P("tensor", None),
        P(),
        P(),
        P(),
        P(None, "tensor"),
        P("tensor"),
        P("tensor", None),
        P(),
        P(("outer", "inner")),
        P(("outer", "inner"), None, None),
    )
    return jax.shard_map(
        per_device,
        mesh=mesh,
        in_specs=placed,
        out_specs=(
            P(("outer", "inner"), None, None),
            P(("outer", "inner"), None, None),
            P(),
            P(),
            P(None, None, "tensor"),
            P(None, "tensor"),
            P("tensor", None),
            P(),
            P(),
            P(),
            P(None, "tensor"),
            P("tensor"),
            P("tensor", None),
            P(),
        ),
        check_vma=False,
    )
```

profile of v0, /device:TPU:0, one launch (start us, length us, event | category | flops | bytes accessed | tf_op | source)
XLA Modules:
  0.0 1097.4 jit_solution(336543928301203086)
XLA Ops:
  7.3 3.7 convert_reduce_fusion.1
  18.1 5.7 add_convert_fusion.3
  29.5 4.2 fusion.4
  67.0 4.2 fusion.34
  71.5 4.8 copy.109
  76.3 3.8 fusion.28
  83.7 4.9 reshape.226
  88.7 5.1 reshape.230
  93.8 74.9 %all-reduce.16.cloned.1.call-done = f32[1154,1024]{1,0:T(8,128)} async-done(((f32[1154,1024]{1,0:T(8,128)}), f32[1154,1024]{1,0:T(8,128)}) %all-reduce.16.cloned.1.call-update) | async-done | bytes 4726800 | tf_op jit(solution)/shard_map/psum | solution.py:90
  168.6 4.4 fusion.32
  179.4 4.6 convert_reduce_fusion
  185.4 4.3 fusion.35
  189.8 94.8 %all-reduce.18.cloned.1.call-done = f32[1154,1024]{1,0:T(8,128)} async-done(((f32[1154,1024]{1,0:T(8,128)}), f32[1154,1024]{1,0:T(8,128)}) %all-reduce.18.cloned.1.call-update) | async-done | bytes 4726800 | tf_op jit(solution)/shard_map/psum | solution.py:106
  284.6 5.4 multiply_reduce_fusion.2
  290.1 3.9 fusion.31
  298.8 8.5 fusion.26
  307.4 8.8 fusion.15
  316.2 4.2 convolution_convert_fusion
  326.1 8.4 convert_reduce_fusion.2
  339.9 8.1 multiply_reduce_fusion
  348.0 6.5 multiply_convert_fusion
  363.6 4.8 convert_reduce_fusion.3
  376.3 5.7 fusion.2
  382.1 51.6 %reduce-scatter.14.cloned.1.call-done = f32[1024,512]{1,0:T(8,128)} async-done(((f32[1024,1024]{1,0:T(8,128)}), f32[1024,512]{1,0:T(8,128)}) %reduce-scatter.14.cloned.1.call-update) | async-done | bytes 2097168 | tf_op jit(solution)/shard_map/reduce_scatter | solution.py:155
  433.7 46.1 %reduce-scatter.8.cloned.1.call-done = f32[512,3,256]{2,0,1:T(8,128)} async-done(((f32[1024,3,256]{2,0,1:T(8,128)}), f32[512,3,256]{2,0,1:T(8,128)}) %reduce-scatter.8.cloned.1.call-update) | async-done | bytes 1572880 | tf_op jit(solution)/shard_map/reduce_scatter | solution.py:147
  479.9 6.7 fusion.27
  487.7 6.8 convolution_bitcast_fusion
  494.6 210.7 %all-reduce.22.cloned.1.call-done = (f32[512,3,256]{2,0,1:T(8,128)}, f32[256,512]{1,0:T(8,128)}, f32[512,1024]{1,0:T(8,128)}, f32[1024,512]{1,0:T(8,128)}) async-done(((f32[512,3,256]{2,0,1:T(8,128)}, f32[256,512]{1,0:T(8,128)}, f32[512,1024]{1,0:T(8,128)}, f32[1024,512]{1,0:T(8,128)}), (f32[512,3,256]{2,0,1:T(8,128)}, f32[256,512]{1,0:T(8,128)}, f32[512,1024]{1,0:T(8,128)}, ...) | async-done | bytes 6291472 | tf_op jit(solution)/shard_map/psum | solution.py:158
  709.0 8.4 reduce-scatter.16.cloned.1.call-done
  718.3 172.7 %all-reduce.20.cloned.1.call-done = (f32[1154,1024]{1,0:T(8,128)}, f32[1154,1024]{1,0:T(8,128)}) async-done(((f32[1154,1024]{1,0:T(8,128)}, f32[1154,1024]{1,0:T(8,128)}), (f32[1154,1024]{1,0:T(8,128)}, f32[1154,1024]{1,0:T(8,128)})) %all-reduce.20.cloned.1.call-update) | async-done | bytes 9453584 | tf_op jit(solution)/shard_map/psum | solution.py:95
  891.0 6.5 add_convert_fusion.1
  901.2 5.7 copy.140
  906.9 4.3 multiply_reduce_fusion.3
  911.1 8.3 all-reduce.10
  920.0 18.8 %all-reduce.8 = (f32[512]{0:T(512)S(1)}, f32[512]{0:T(512)S(1)}, f32[2,128]{1,0:T(2,128)S(1)}, f32[512]{0:T(512)S(1)}, f32[512]{0:T(512)S(1)}, /*index=5*/f32[512]{0:T(512)S(1)}, f32[512]{0:T(512)S(1)}, f32[512]{0:T(512)S(1)}) all-reduce(f32[512]{0:T(512)S(1)} %dynamic-slice.1, ...), channel_id=1, replica_groups=mesh['outer'=4,'inner'=2,'tensor'=4] {'outer'}, use_global_device_ids=true, to_apply=%region_17.0 | all-reduce | flops 3840 | bytes 30720 | tf_op jit(solution)/shard_map/psum | solution.py:158
  938.8 4.5 all-gather.1
  943.3 4.5 all-gather
  947.9 4.4 all_gather.39
  952.2 4.5 all-gather.2
  956.8 4.4 all-gather.3
  961.1 4.4 all-gather.4
  965.5 4.4 all-gather.5
  969.8 4.6 all-gather.6
  974.5 5.0 fusion.30
  985.0 5.5 copy.141
  990.5 28.3 %all-gather.16.cloned.1.call-done = f32[1024,1024]{1,0:T(8,128)} async-done(((f32[512,1024]{1,0:T(8,128)}), f32[1024,1024]{1,0:T(8,128)}) %all-gather.16.cloned.1.call-update) | async-done | bytes 4194320 | tf_op jit(solution)/shard_map/all_gather | solution.py:198
  1018.8 58.3 %all-gather.18.cloned.1.call-done = f32[1024,1024]{1,0:T(8,128)} async-done(((f32[1024,512]{1,0:T(8,128)}), f32[1024,1024]{1,0:T(8,128)}) %all-gather.18.cloned.1.call-update) | async-done | bytes 4194320 | tf_op jit(solution)/shard_map/all_gather | solution.py:200
  1078.2 3.8 copy.190
  (192 shorter events, 115.1 us)
Async XLA Ops:
  7.2 172.2 %copy-start = (bf16[1024,1024]{1,0:T(8,128)(2,1)S(1)}, bf16[1024,1024]{1,0:T(8,128)(2,1)}, u32[]{:S(2)}) copy-start(bf16[1024,1024]{1,0:T(8,128)(2,1)} %param.26) | copy-start | bytes 6291460
  7.2 10.9 copy-start.18
  7.2 10.9 copy-start.24
  7.2 161.4 %all-reduce.16.cloned.1.call-start = ((), (), s32[]{:S(2)}) async-start(), calls=%async_computation.5 | async-start | bytes 9502720 | tf_op jit(solution)/shard_map/psum | solution.py:90
  7.3 3.8 copy-start.5
  11.0 12.8 %copy-start.11 = (f32[2,577]{0,1:T(8,128)}, f32[2,577]{0,1:T(8,128)S(1)}, u32[]{:S(2)}) copy-start(f32[2,577]{0,1:T(8,128)S(1)} %broadcast_multiply_fusion) | copy-start | bytes 13852
  56.0 4.4 copy-start.1
  71.2 5.0 copy-start.29
  71.2 213.4 %all-reduce.18.cloned.1.call-start = ((), (), s32[]{:S(2)}) async-start(), calls=%async_computation.6 | async-start | bytes 9502720 | tf_op jit(solution)/shard_map/psum | solution.py:106
  71.5 4.8 copy-start.15
  88.7 80.0 %copy-start.22 = (f32[1024]{0:T(1024)S(1)}, f32[1024]{0:T(1024)}, u32[]{:S(2)}) copy-start(f32[1024]{0:T(1024)} %param.21) | copy-start | bytes 12292
  173.0 6.3 copy-start.2
  173.1 3.2 copy-start.26
  173.1 3.2 copy-start.27
  173.1 3.2 copy-start.28
  173.1 6.3 slice-start.2
  176.2 3.1 slice-start.3
  179.4 4.6 copy-start.31
  189.8 192.3 %reduce-scatter.10.cloned.1.call-start = ((), (), s32[]{:S(2)}) async-start(), calls=%async_computation.9 | async-start | bytes 1572864 | tf_op jit(solution)/shard_map/reduce_scatter | solution.py:149
  284.6 5.5 copy-start.7
  284.6 9.4 slice-start.4
  290.1 3.9 slice-start.5
  294.1 2.8 copy-start.9
  294.7 2.2 copy-start.3
  298.7 83.4 %reduce-scatter.12.cloned.1.call-start = ((), (), s32[]{:S(2)}) async-start(), calls=%async_computation.11 | async-start | bytes 6291456 | tf_op jit(solution)/shard_map/reduce_scatter | solution.py:153
  307.3 126.4 %reduce-scatter.14.cloned.1.call-start = ((), (), s32[]{:S(2)}) async-start(), calls=%async_computation.13 | async-start | bytes 6291456 | tf_op jit(solution)/shard_map/reduce_scatter | solution.py:155
  316.2 163.6 %reduce-scatter.8.cloned.1.call-start = ((), (), s32[]{:S(2)}) async-start(), calls=%async_computation.7 | async-start | bytes 4718592 | tf_op jit(solution)/shard_map/reduce_scatter | solution.py:147
  348.0 9.1 copy-start.8
  354.5 2.6 copy-start.4
  357.1 6.5 copy-start.10
  382.0 323.3 %all-reduce.22.cloned.1.call-start = ((), (), s32[]{:S(2)}) async-start(), calls=%async_computation.17 | async-start | bytes 12582912 | tf_op jit(solution)/shard_map/psum | solution.py:158
  479.9 237.6 %reduce-scatter.16.cloned.1.call-start = ((), (), s32[]{:S(2)}) async-start(), calls=%async_computation.15 | async-start | bytes 196608
  487.6 403.3 %all-reduce.20.cloned.1.call-start = ((), (), s32[]{:S(2)}) async-start(), calls=%async_computation.16 | async-start | bytes 19005440 | tf_op jit(solution)/shard_map/psum | solution.py:95
  494.5 212.9 %copy-start.12 = (f32[2,577]{0,1:T(8,128)S(1)}, f32[2,577]{0,1:T(8,128)}, u32[]{:S(2)}) copy-start(f32[2,577]{0,1:T(8,128)} %copy-done.11) | copy-start | bytes 13852
  494.5 213.1 %copy-start.20 = (f32[2,577]{1,0:T(2,128)S(1)}, f32[2,577]{1,0:T(2,128)}, u32[]{:S(2)}) copy-start(f32[2,577]{1,0:T(2,128)} %get-tuple-element.111) | copy-start | bytes 13852
  494.6 213.2 %copy-start.30 = (u32[32]{0:T(128)S(1)}, u32[32]{0:T(128)}, u32[]{:S(2)}) copy-start(u32[32]{0:T(128)} %constant.32) | copy-start | bytes 388
  494.6 396.4 %copy-start.23 = (f32[1024]{0:T(1024)S(1)}, f32[1024]{0:T(1024)}, u32[]{:S(2)}) copy-start(f32[1024]{0:T(1024)} %param.27) | copy-start | bytes 12292
  494.6 495.9 %all-gather.14.cloned.1.call-start = ((), (), s32[]{:S(2)}) async-start(), calls=%async_computation.10 | async-start | bytes 1572864 | tf_op jit(solution)/shard_map/all_gather | solution.py:194
  705.4 285.1 %all-gather.12.cloned.1.call-start = ((), (), s32[]{:S(2)}) async-start(), calls=%async_computation.8 | async-start | bytes 4718592 | tf_op jit(solution)/shard_map/all_gather | solution.py:192
  706.1 312.7 %all-gather.16.cloned.1.call-start = ((), (), s32[]{:S(2)}) async-start(), calls=%async_computation.12 | async-start | bytes 6291456 | tf_op jit(solution)/shard_map/all_gather | solution.py:198
  706.7 370.4 %all-gather.18.cloned.1.call-start = ((), (), s32[]{:S(2)}) async-start(), calls=%async_computation.14 | async-start | bytes 6291456 | tf_op jit(solution)/shard_map/all_gather | solution.py:200
  897.5 9.4 copy-start.19
  901.2 5.7 copy-start.6
  906.8 72.7 %slice-start = ((s8[4751360]{0:T(1024)(128)(4,1)}), s8[557056]{0:T(1024)(128)(4,1)S(1)}, s32[]{:S(2)}) async-start(s8[4751360]{0:T(1024)(128)(4,1)} %bitcast.68), calls=%async_computation.18 | async-start | bytes 1114112
  974.5 5.1 slice-start.1
  990.5 92.1 %copy-start.16 = (f32[256,1024]{1,0:T(8,128)S(1)}, f32[256,1024]{1,0:T(8,128)}, u32[]{:S(2)}) copy-start(f32[256,1024]{1,0:T(8,128)} %all-gather.14.cloned.1.call-done) | copy-start | bytes 3145732
  1077.1 8.4 copy-start.13
  1082.7 5.4 copy-start.14
  (4 other events, 5.4 us)
Sparse Core Ops, SparseCore 0:
  71.3 97.2 all-reduce.15
  189.9 94.6 all-reduce.17
  298.8 20.5 reduce-scatter.9
  322.1 54.3 reduce-scatter.11
  379.3 54.3 reduce-scatter.13
  436.4 43.4 reduce-scatter.7
  482.4 222.8 all-reduce.21
  708.1 9.2 reduce-scatter.15
  720.0 170.9 all-reduce.19
  892.4 21.4 all-gather.13
  915.4 45.1 all-gather.11
  962.0 56.7 all-gather.15
  1020.3 56.6 all-gather.17
where the time goes:
time: 1100 us
  waiting for transfers between devices  748 us (68%)
  local copies, waits for them, and re-layouts  120 us (11%)
  matrix products  92 us (8%)
  blocking collectives  62.8 us (6%)
  other arithmetic  58.5 us (5%)
  between operations  15.5 us (1%)
    psum x1, waiting for transfers between devices, per_device(): lax.psum((shares[0], shares[1], shares[2], shares[3], shares[4], shares[5...  211 us
    psum x1, waiting for transfers between devices, per_device(): mlp_total = lax.psum(mat_prod(gelu_out, w_fc2), 'tensor')  173 us
    psum x1, waiting for transfers between devices, per_device(): norm2_grad = lax.psum(right_contract(pre_grad, w_fc1), 'tensor')  94.8 us
    psum x1, waiting for transfers between devices, per_device(): attn_total = lax.psum(mat_prod(attended, w_out), 'tensor')  74.9 us
    all_gather x1, waiting for transfers between devices, per_device(): lax.all_gather(s_w_fc2, 'inner', axis=1, tiled=True)  58.3 us
    reduce_scatter x1, waiting for transfers between devices, per_device(): lax.psum_scatter(g_w_fc2, 'inner', scatter_dimension=1, tiled=True)  51.6 us
    reduce_scatter x1, waiting for transfers between devices, per_device(): lax.psum_scatter(g_w_qkv, 'inner', scatter_dimension=0, tiled=True)  46.1 us
    unnamed x106, local copies, waits for them, and re-layouts  45.1 us
  transfers between devices with their start and end apart: 13, of which 9 were waited for; matrix products, arithmetic and copies ran while one was open for 14% of the time, Pallas kernels for 0%

commit v1 on v0

--- a/solution.py
+++ b/solution.py
@@ -87,7 +87,7 @@
         "bhqk,bkhd->bqhd", attn_probs, v_heads, preferred_element_type=jnp.float32
     )
     attended = attended.astype(jnp.bfloat16).reshape(row_count, head_cols)
-    attn_total = lax.psum(mat_prod(attended, w_out), "tensor")
+    attn_total = jnp.sum(lax.all_gather(mat_prod(attended, w_out), "tensor"), axis=0)
     resid_mid = x_rows + attn_total + out_bias
     normed2 = layer_norm(resid_mid, ln2_gain, ln2_shift).astype(jnp.bfloat16)
     pre_act = mat_prod(normed2, w_fc1) + fc1_bias

time: 1100 us -> 1150 us (1.045)
  waiting for transfers between devices: 748 us -> 772 us
  other arithmetic: 58.5 us -> 80.7 us
    all_gather x0 -> x1, waiting for transfers between devices: none -> 96.9 us  [per_device(): lax.all_gather(mat_prod(attended, w_out), 'tensor')]
    psum x1 -> x0, waiting for transfers between devices: 74.9 us -> none  [per_device(): attn_total = lax.psum(mat_prod(attended, w_out), 'tensor')]
    unnamed x106 -> x109, local copies, waits for them, and re-layouts: 45.1 us -> 43 us
where the time goes in v1:
time: 1150 us; the launch traced here: 1140 us
  waiting for transfers between devices  772 us (67%)
  local copies, waits for them, and re-layouts  115 us (10%)
  matrix products  94 us (8%)
  other arithmetic  80.7 us (7%)
  blocking collectives  62.6 us (5%)
  between operations  15.4 us (1%)
    psum x1, waiting for transfers between devices, per_device(): lax.psum((shares[0], shares[1], shares[2], shares[3], shares[4], shares[5...  211 us
    psum x1, waiting for transfers between devices, per_device(): mlp_total = lax.psum(mat_prod(gelu_out, w_fc2), 'tensor')  173 us
    all_gather x1, waiting for transfers between devices, per_device(): lax.all_gather(mat_prod(attended, w_out), 'tensor')  96.9 us
    psum x1, waiting for transfers between devices, per_device(): norm2_grad = lax.psum(right_contract(pre_grad, w_fc1), 'tensor')  94.7 us
    all_gather x1, waiting for transfers between devices, per_device(): lax.all_gather(s_w_fc2, 'inner', axis=1, tiled=True)  58.3 us
    reduce_scatter x1, waiting for transfers between devices, per_device(): lax.psum_scatter(g_w_fc2, 'inner', scatter_dimension=1, tiled=True)  53.8 us
    reduce_scatter x1, waiting for transfers between devices, per_device(): lax.psum_scatter(g_w_qkv, 'inner', scatter_dimension=0, tiled=True)  46.1 us
    unnamed x109, local copies, waits for them, and re-layouts  43 us
  transfers between devices with their start and end apart: 13, of which 9 were waited for; matrix products, arithmetic and copies ran while one was open for 14% of the time, Pallas kernels for 0%

profile of v1, /device:TPU:0, one launch (start us, length us, event | category | flops | bytes accessed | tf_op | source)
XLA Modules:
  0.0 1141.4 jit_solution(10656330114735585893)
XLA Ops:
  22.6 4.2 fusion.5
  59.5 4.0 convolution_bitcast_fusion.1
  64.0 5.8 fusion.28
  73.8 6.1 reshape.255
  79.9 4.9 copy_convert_fusion
  84.8 5.4 reshape.259
  90.2 96.9 %all-gather.23.cloned.1.call-done = f32[4,1154,1024]{2,1,0:T(8,128)} async-done(((f32[1,1154,1024]{2,1,0:T(8,128)}), f32[4,1154,1024]{2,1,0:T(8,128)}) %all-gather.23.cloned.1.call-update) | async-done | bytes 18907152 | tf_op jit(solution)/shard_map/all_gather | solution.py:90
  187.1 11.5 %reduce_sum.183 = f32[1154,1024]{1,0:T(8,128)} reduce(f32[4,1154,1024]{2,1,0:T(8,128)} %all-gather.23.cloned.1.call-done, f32[]{:T(128)} %constant.8.clone.1), dimensions={0}, to_apply=%region_4.0 | reduce | flops 3545088 | bytes 23633924 | tf_op jit(solution)/shard_map/reduce_sum | solution.py:90
  198.6 5.0 reduce_sum.184
  203.6 4.2 fusion.2
  210.1 7.6 add_add_fusion.4
  217.9 5.9 convolution_add_fusion
  223.8 4.4 convert_reduce_fusion
  229.6 4.4 fusion.33
  234.1 94.7 %all-reduce.15.cloned.1.call-done = f32[1154,1024]{1,0:T(8,128)} async-done(((f32[1154,1024]{1,0:T(8,128)}), f32[1154,1024]{1,0:T(8,128)}) %all-reduce.15.cloned.1.call-update) | async-done | bytes 4726800 | tf_op jit(solution)/shard_map/psum | solution.py:106
  328.7 5.4 multiply_reduce_fusion.4
  342.8 8.5 fusion.26
  351.4 8.8 fusion.16
  360.3 4.0 convolution_convert_fusion
  368.4 8.4 convert_reduce_fusion.2
  382.1 7.8 multiply_reduce_fusion
  389.9 6.4 multiply_convert_fusion
  405.4 4.7 convert_reduce_fusion.3
  418.1 5.7 fusion.3
  423.8 53.8 %reduce-scatter.14.cloned.1.call-done = f32[1024,512]{1,0:T(8,128)} async-done(((f32[1024,1024]{1,0:T(8,128)}), f32[1024,512]{1,0:T(8,128)}) %reduce-scatter.14.cloned.1.call-update) | async-done | bytes 2097168 | tf_op jit(solution)/shard_map/reduce_scatter | solution.py:155
  477.7 46.1 %reduce-scatter.8.cloned.1.call-done = f32[512,3,256]{2,0,1:T(8,128)} async-done(((f32[1024,3,256]{2,0,1:T(8,128)}), f32[512,3,256]{2,0,1:T(8,128)}) %reduce-scatter.8.cloned.1.call-update) | async-done | bytes 1572880 | tf_op jit(solution)/shard_map/reduce_scatter | solution.py:147
  523.9 6.8 fusion.27
  531.7 6.8 convolution_bitcast_fusion
  538.6 210.7 %all-reduce.19.cloned.1.call-done = (f32[512,3,256]{2,0,1:T(8,128)}, f32[256,512]{1,0:T(8,128)}, f32[512,1024]{1,0:T(8,128)}, f32[1024,512]{1,0:T(8,128)}) async-done(((f32[512,3,256]{2,0,1:T(8,128)}, f32[256,512]{1,0:T(8,128)}, f32[512,1024]{1,0:T(8,128)}, f32[1024,512]{1,0:T(8,128)}), (f32[512,3,256]{2,0,1:T(8,128)}, f32[256,512]{1,0:T(8,128)}, f32[512,1024]{1,0:T(8,128)}, ...) | async-done | bytes 6291472 | tf_op jit(solution)/shard_map/psum | solution.py:158
  752.9 8.6 reduce-scatter.16.cloned.1.call-done
  762.3 172.7 %all-reduce.17.cloned.1.call-done = (f32[1154,1024]{1,0:T(8,128)}, f32[1154,1024]{1,0:T(8,128)}) async-done(((f32[1154,1024]{1,0:T(8,128)}, f32[1154,1024]{1,0:T(8,128)}), (f32[1154,1024]{1,0:T(8,128)}, f32[1154,1024]{1,0:T(8,128)})) %all-reduce.17.cloned.1.call-update) | async-done | bytes 9453584 | tf_op jit(solution)/shard_map/psum | solution.py:95
  935.0 6.5 add_convert_fusion.2
  945.2 5.7 copy.130
  950.9 4.3 multiply_reduce_fusion.5
  955.2 8.3 all-reduce.10
  964.0 18.8 %all-reduce.8 = (f32[512]{0:T(512)S(1)}, f32[512]{0:T(512)S(1)}, f32[2,128]{1,0:T(2,128)S(1)}, f32[512]{0:T(512)S(1)}, f32[512]{0:T(512)S(1)}, /*index=5*/f32[512]{0:T(512)S(1)}, f32[512]{0:T(512)S(1)}, f32[512]{0:T(512)S(1)}) all-reduce(f32[512]{0:T(512)S(1)} %dynamic-slice.1, ...), channel_id=1, replica_groups=mesh['outer'=4,'inner'=2,'tensor'=4] {'outer'}, use_global_device_ids=true, to_apply=%region_17.0 | all-reduce | flops 3840 | bytes 30720 | tf_op jit(solution)/shard_map/psum | solution.py:158
  982.8 4.5 all-gather.3
  987.4 4.5 all-gather.2
  991.9 4.4 all_gather.47
  996.3 4.5 all-gather.4
  1000.8 4.4 all-gather.5
  1005.2 4.4 all-gather.6
  1009.5 4.4 all-gather.7
  1013.9 4.4 all-gather.8
  1018.3 5.1 fusion.30
  1028.8 5.5 copy.131
  1034.4 28.4 %all-gather.19.cloned.1.call-done = f32[1024,1024]{1,0:T(8,128)} async-done(((f32[512,1024]{1,0:T(8,128)}), f32[1024,1024]{1,0:T(8,128)}) %all-gather.19.cloned.1.call-update) | async-done | bytes 4194320 | tf_op jit(solution)/shard_map/all_gather | solution.py:198
  1062.8 58.3 %all-gather.21.cloned.1.call-done = f32[1024,1024]{1,0:T(8,128)} async-done(((f32[1024,512]{1,0:T(8,128)}), f32[1024,1024]{1,0:T(8,128)}) %all-gather.21.cloned.1.call-update) | async-done | bytes 4194320 | tf_op jit(solution)/shard_map/all_gather | solution.py:200
  (198 shorter events, 119.5 us)
Async XLA Ops:
  7.2 216.6 %copy-start = (bf16[1024,1024]{1,0:T(8,128)(2,1)S(1)}, bf16[1024,1024]{1,0:T(8,128)(2,1)}, u32[]{:S(2)}) copy-start(bf16[1024,1024]{1,0:T(8,128)(2,1)} %param.26) | copy-start | bytes 6291460
  7.2 8.3 copy-start.20
  7.2 8.3 copy-start.25
  7.2 179.9 %all-gather.23.cloned.1.call-start = ((), (), s32[]{:S(2)}) async-start(), calls=%async_computation.14 | async-start | bytes 23756800 | tf_op jit(solution)/shard_map/all_gather | solution.py:90
  9.8 9.3 copy-start.17
  38.9 12.4 %copy-start.8 = (f32[2,577,4,64]{1,3,2,0:T(8,128)}, f32[2,577,4,64]{1,3,2,0:T(8,128)S(1)}, u32[]{:S(2)}) copy-start(f32[2,577,4,64]{1,3,2,0:T(8,128)S(1)} %copy.107) | copy-start | bytes 3545092
  49.2 4.4 copy-start.1
  59.5 4.5 copy-start.31
  63.5 265.2 %all-reduce.15.cloned.1.call-start = ((), (), s32[]{:S(2)}) async-start(), calls=%async_computation.5 | async-start | bytes 9502720 | tf_op jit(solution)/shard_map/psum | solution.py:106
  198.6 5.0 copy-start.19
  203.6 4.2 copy-start.2
  203.6 5.2 copy-start.5
  210.1 7.7 copy-start.24
  210.1 7.7 copy-start.29
  210.1 7.7 copy-start.30
  210.1 13.7 %slice-start.2 = ((s8[4751360]{0:T(1024)(128)(4,1)}), s8[557056]{0:T(1024)(128)(4,1)S(1)}, s32[]{:S(2)}) async-start(s8[4751360]{0:T(1024)(128)(4,1)} %bitcast.72), calls=%async_computation.20 | async-start | bytes 1114112
  217.9 5.9 slice-start.3
  223.8 4.4 copy-start.33
  223.8 5.8 copy-start.28
  234.0 189.8 %reduce-scatter.10.cloned.1.call-start = ((), (), s32[]{:S(2)}) async-start(), calls=%async_computation.8 | async-start | bytes 1572864 | tf_op jit(solution)/shard_map/reduce_scatter | solution.py:149
  328.7 5.5 copy-start.7
  328.7 9.4 slice-start.4
  342.7 81.1 %reduce-scatter.12.cloned.1.call-start = ((), (), s32[]{:S(2)}) async-start(), calls=%async_computation.10 | async-start | bytes 6291456 | tf_op jit(solution)/shard_map/reduce_scatter | solution.py:153
  351.3 9.0 copy-start.14
  351.3 126.4 %reduce-scatter.14.cloned.1.call-start = ((), (), s32[]{:S(2)}) async-start(), calls=%async_computation.12 | async-start | bytes 6291456 | tf_op jit(solution)/shard_map/reduce_scatter | solution.py:155
  360.2 163.6 %reduce-scatter.8.cloned.1.call-start = ((), (), s32[]{:S(2)}) async-start(), calls=%async_computation.6 | async-start | bytes 4718592 | tf_op jit(solution)/shard_map/reduce_scatter | solution.py:147
  368.4 13.8 %copy-start.9 = (f32[2,577,4,64]{1,3,2,0:T(8,128)S(1)}, f32[2,577,4,64]{1,3,2,0:T(8,128)}, u32[]{:S(2)}) copy-start(f32[2,577,4,64]{1,3,2,0:T(8,128)} %copy-done.8) | copy-start | bytes 3545092
  389.9 9.0 copy-start.10
  398.9 6.5 copy-start.11
  423.7 325.6 %all-reduce.19.cloned.1.call-start = ((), (), s32[]{:S(2)}) async-start(), calls=%async_computation.17 | async-start | bytes 12582912 | tf_op jit(solution)/shard_map/psum | solution.py:158
  523.9 237.6 %reduce-scatter.16.cloned.1.call-start = ((), (), s32[]{:S(2)}) async-start(), calls=%async_computation.15 | async-start | bytes 196608
  531.7 403.3 %all-reduce.17.cloned.1.call-start = ((), (), s32[]{:S(2)}) async-start(), calls=%async_computation.16 | async-start | bytes 19005440 | tf_op jit(solution)/shard_map/psum | solution.py:95
  538.5 212.9 %copy-start.18 = (f32[2,577]{1,0:T(2,128)S(1)}, f32[2,577]{1,0:T(2,128)}, u32[]{:S(2)}) copy-start(f32[2,577]{1,0:T(2,128)} %copy-done.17) | copy-start | bytes 13852
  538.5 213.0 %copy-start.22 = (f32[2,577]{1,0:T(2,128)S(1)}, f32[2,577]{1,0:T(2,128)}, u32[]{:S(2)}) copy-start(f32[2,577]{1,0:T(2,128)} %get-tuple-element.109) | copy-start | bytes 13852
  538.5 213.1 %copy-start.32 = (u32[32]{0:T(128)S(1)}, u32[32]{0:T(128)}, u32[]{:S(2)}) copy-start(u32[32]{0:T(128)} %constant.32) | copy-start | bytes 388
  538.6 396.5 %copy-start.26 = (f32[1024]{0:T(1024)S(1)}, f32[1024]{0:T(1024)}, u32[]{:S(2)}) copy-start(f32[1024]{0:T(1024)} %param.27) | copy-start | bytes 12292
  538.6 495.8 %all-gather.17.cloned.1.call-start = ((), (), s32[]{:S(2)}) async-start(), calls=%async_computation.9 | async-start | bytes 1572864 | tf_op jit(solution)/shard_map/all_gather | solution.py:194
  749.4 285.0 %all-gather.15.cloned.1.call-start = ((), (), s32[]{:S(2)}) async-start(), calls=%async_computation.7 | async-start | bytes 4718592 | tf_op jit(solution)/shard_map/all_gather | solution.py:192
  750.1 312.7 %all-gather.19.cloned.1.call-start = ((), (), s32[]{:S(2)}) async-start(), calls=%async_computation.11 | async-start | bytes 6291456 | tf_op jit(solution)/shard_map/all_gather | solution.py:198
  750.7 370.4 %all-gather.21.cloned.1.call-start = ((), (), s32[]{:S(2)}) async-start(), calls=%async_computation.13 | async-start | bytes 6291456 | tf_op jit(solution)/shard_map/all_gather | solution.py:200
  941.5 9.4 copy-start.21
  945.2 5.7 copy-start.6
  950.9 4.3 copy-start.23
  950.9 72.5 %slice-start = ((s8[4751360]{0:T(1024)(128)(4,1)}), s8[557056]{0:T(1024)(128)(4,1)S(1)}, s32[]{:S(2)}) async-start(s8[4751360]{0:T(1024)(128)(4,1)} %bitcast.70), calls=%async_computation.18 | async-start | bytes 1114112
  1018.3 5.1 slice-start.1
  1034.4 92.3 %copy-start.15 = (f32[256,1024]{1,0:T(8,128)S(1)}, f32[256,1024]{1,0:T(8,128)}, u32[]{:S(2)}) copy-start(f32[256,1024]{1,0:T(8,128)} %all-gather.17.cloned.1.call-done) | copy-start | bytes 3145732
  1121.1 8.4 copy-start.12
  1126.7 5.4 copy-start.13
  (6 other events, 13.3 us)
Sparse Core Ops, SparseCore 0:
  63.7 123.4 all-gather.22
  234.1 94.5 all-reduce.14
  342.8 20.5 reduce-scatter.9
  366.2 54.3 reduce-scatter.11
  423.3 54.3 reduce-scatter.13
  480.4 43.4 reduce-scatter.7
  526.5 222.8 all-reduce.18
  752.1 9.2 reduce-scatter.15
  764.0 170.9 all-reduce.16
  936.4 21.4 all-gather.16
  959.4 45.1 all-gather.14
  1006.0 56.7 all-gather.18
  1064.3 56.6 all-gather.20
